TPU v7x, 128 devices: a whole 4x4x4 slice. The times are simulated.
128 devices in a mesh: wave: 16 (over y, z_lo, core), pole: 8 (over x, z_hi).
Axes of the slice: x: 4, y: 4, z: 4 (z_hi: 2, z_lo: 2; z = z_hi * 2 + z_lo), core: 2. Of those that a mesh axis runs over, the one named last changes fastest.
Arguments:
- grid: float32 [6, 256, 3072], P(None, None, 'wave'), may hold values from -6 to 6
- legendre: bfloat16 [256, 2, 1536, 1024], P('wave', None, None, 'pole'), may hold values from -0.15625 to 0.15625
- wave_table: int32 [256], replicated, may hold values from 0 to 255, each once
- pole_table: float32 [4, 64], replicated, may hold values from -1.5 to 2.5, as said below
- pole_index: int32 [32], replicated, may hold values from 0 to 63
Outputs:
- next_state: float32 [6, 2, 256, 1024], P(None, None, 'wave', 'pole')
Inputs may be any that keep to these rules, and one draw needn't show every extreme that they name: Slot s holds zonal wavenumber wave_table[s], every wavenumber of 0 to 255 once; row s of legendre belongs to it. `pole_table`: shift real parts lie in 1.5 to 2.5, shift imaginary parts in -1.5 to 1.5, weights in -1.2 to 1.2.
All inputs are finite; a program needn't handle non-finite values.
Results may differ from a plain program's by a relative error of at most 0.0003.
Values sent between devices are 32-bit elements; how exact they have to be, the bound alone decides.
No kernel may reach another device: no remote copies, remote signals or barrier semaphores. Data moves between devices by JAX's collectives and lax.ppermute only.
A program may use at most 128 MiB of HBM per device.

v0:
```python
import jax
import jax.numpy as jnp
from jax import lax
from jax.sharding import PartitionSpec as P

SWEEPS = 8
coriolis_step = 1.2
gravity_step = 0.0008


def split_high(values):
    upper_part = values.astype(jnp.bfloat16)
    kept = lax.optimization_barrier(upper_part)
    lower_part = (values - kept.astype(jnp.float32)).astype(jnp.bfloat16)
    return (upper_part, lower_part)


def coefficients(wavenum, count):
    index = jnp.arange(count, dtype=jnp.int32).astype(jnp.float32)
    parity = jnp.arange(2, dtype=jnp.int32).astype(jnp.float32)
    order = (2.0 * index[None, :] + parity[:, None])[:, None, :]
    wave = wavenum[None, :, None]
    degree = wave + order
    product = degree * (degree + 1.0)
    rossby = coriolis_step * wave / jnp.maximum(product, 2.0)
    gravity = gravity_step * jnp.sqrt(product)
    e_lo = jnp.sqrt(order * (2.0 * wave + order) / jnp.maximum(4.0 * degree * degree - 1.0, 1.0))
    after = order + 1.0
    upper_deg = degree + 1.0
    e_hi = jnp.sqrt(
        after * (2.0 * wave + after) / jnp.maximum(4.0 * upper_deg * upper_deg - 1.0, 1.0)
    )
    return (e_lo, e_hi, rossby, gravity)


def cmul(are, aim, bre, bim):
    return (are * bre - aim * bim, are * bim + aim * bre)


def zero_extend(field):
    return jnp.pad(field, ((0, 0), (0, 0), (0, 0), (0, 0), (1, 1)))


def solve(spectra, coef, shifts, extend):
    e_lo, e_hi, rossby, gravity = coef
    count = spectra.shape[3]
    shift_re = shifts[:, 0][:, None, None, None]
    shift_im = shifts[:, 1][:, None, None, None]
    weight_re = shifts[:, 2][:, None, None, None]
    weight_im = shifts[:, 3][:, None, None, None]
    z0r, z0i = (spectra[0][None], spectra[1][None])
    d0r, d0i = (spectra[2][None], spectra[3][None])
    h0r, h0i = (spectra[4][None], spectra[5][None])
    b_re = shift_re + 0.0 * rossby[None]
    b_im = shift_im + rossby[None]
    b_mag = b_re * b_re + b_im * b_im
    inv_re, inv_im = (b_re / b_mag, -b_im / b_mag)
    det_re, det_im = cmul(b_re, b_im, shift_re, shift_im)
    det_re = det_re + gravity[None] * gravity[None]
    det_mag = det_re * det_re + det_im * det_im
    dinv_re, dinv_im = (det_re / det_mag, -det_im / det_mag)
    grav = gravity[None]
    hb_re, hb_im = cmul(b_re, b_im, h0r, h0i)
    zr, zi, dr, di, hr, hi = (z0r, z0i, d0r, d0i, h0r, h0i)
    for sweep in range(SWEEPS):
        if sweep == 0:
            rzr, rzi, rdr, rdi = (z0r, z0i, d0r, d0i)
        else:
            both = jnp.stack([zr, zi, dr, di], axis=0)
            ext = extend(both)
            lower = jnp.stack([ext[:, :, 1, :, 0:count], ext[:, :, 0, :, 1 : count + 1]], axis=2)
            upper = jnp.stack(
                [ext[:, :, 1, :, 1 : count + 1], ext[:, :, 0, :, 2 : count + 2]], axis=2
            )
            near = e_lo * lower + e_hi * upper
            rzr = z0r - coriolis_step * near[2]
            rzi = z0i - coriolis_step * near[3]
            rdr = d0r + coriolis_step * near[0]
            rdi = d0i + coriolis_step * near[1]
        zr, zi = cmul(rzr, rzi, inv_re, inv_im)
        nd_re, nd_im = cmul(shift_re, shift_im, rdr, rdi)
        nd_re = nd_re + grav * h0r
        nd_im = nd_im + grav * h0i
        nh_re = hb_re - grav * rdr
        nh_im = hb_im - grav * rdi
        dr, di = cmul(nd_re, nd_im, dinv_re, dinv_im)
        hr, hi = cmul(nh_re, nh_im, dinv_re, dinv_im)
    parts = []
    for field_re, field_im in ((zr, zi), (dr, di), (hr, hi)):
        out_re, out_im = cmul(weight_re, weight_im, field_re, field_im)
        parts.append(jnp.sum(out_re, axis=0))
        parts.append(jnp.sum(out_im, axis=0))
    return jnp.stack(parts, axis=0)


def lookup(pole_table, chosen):
    columns = jnp.arange(pole_table.shape[1], dtype=jnp.int32)
    onehot = (chosen[:, None] == columns[None, :]).astype(jnp.float32)
    return jnp.dot(onehot, jnp.transpose(pole_table), precision=lax.Precision.HIGHEST)


def shards(grid, legendre, wave_table, pole_table, pole_index):
    slots = legendre.shape[0]
    local_k = legendre.shape[3]
    lat_rows = grid.shape[2]
    wave_count = lax.axis_size("wave")
    half_count = wave_count // 2
    columns = jnp.take(grid, wave_table, axis=1)
    regrouped = lax.all_to_all(columns[None], "wave", split_axis=2, concat_axis=0, tiled=True)
    north = regrouped[:half_count]
    south = regrouped[half_count:]
    parts = jnp.stack([north + south, north - south], axis=0)
    high, low = split_high(parts)
    leg_blocks = legendre.reshape(slots, 2, half_count, lat_rows, local_k)
    first = jnp.einsum("mpwlk,pwcml->cpmk", leg_blocks, high, preferred_element_type=jnp.float32)
    second = jnp.einsum("mpwlk,pwcml->cpmk", leg_blocks, low, preferred_element_type=jnp.float32)
    spectra = first + second
    own_waves = lax.dynamic_slice_in_dim(wave_table, lax.axis_index("wave") * slots, slots).astype(
        jnp.float32
    )
    whole = lax.all_gather(spectra, "pole", axis=3, tiled=True)
    per_device = pole_index.shape[0] // lax.axis_size("pole")
    chosen = lax.dynamic_slice_in_dim(pole_index, lax.axis_index("pole") * per_device, per_device)
    coef = coefficients(own_waves, whole.shape[3])
    partial_terms = solve(whole, coef, lookup(pole_table, chosen), zero_extend)
    result = lax.psum_scatter(partial_terms, "pole", scatter_dimension=3, tiled=True)
    return result


def solution(mesh):
    in_specs = (P(None, None, "wave"), P("wave", None, None, "pole"), P(), P(), P())
    out_specs = P(None, None, "wave", "pole")
    return jax.shard_map(shards, mesh=mesh, in_specs=in_specs, out_specs=out_specs, check_vma=False)
```

profile of v0, /device:TPU:0, one launch (start us, length us, event | category | flops | bytes accessed | tf_op | source)
XLA Modules:
  0.0 192.9 jit_solution(7145403172599582811)
XLA Ops:
  6.5 0.7 compare_and_fusion
  7.2 0.7 compare_select_fusion
  7.9 2.8 %copy.19 = f32[6,256,192]{2,0,1:T(8,128)} copy(f32[6,256,192]{1,2,0:T(8,128)} %param.5) | data formatting | bytes 2359296 | tf_op args[0]
  10.8 2.3 %gather_fusion = f32[256,6,192]{2,1,0:T(8,128)S(1)} fusion(f32[6,256,192]{2,0,1:T(8,128)} %copy.19, s32[1024]{0:T(1024)S(1)} %pad_clamp_fusion), kind=kCustom, calls=%fused_computation | custom fusion | bytes 2360320 | tf_op jit(solution)/shard_map/jit(_take)/gather | solution.py:108
  13.1 0.3 bitcast_select_fusion
  13.5 2.8 %copy.20 = f32[1,6,256,192]{3,0,1,2:T(1,128)} copy(f32[1,6,256,192]{3,1,2,0:T(8,128)S(1)} %bitcast_select_fusion) | data formatting | bytes 2359296 | tf_op jit(solution)/shard_map/jit(_take)/select_n | solution.py:108
  16.2 6.1 %all-to-all-start = ((f32[1,6,256,192]{3,0,1,2:T(1,128)}), f32[1,6,256,192]{3,0,1,2:T(1,128)S(1)}, u32[]{:S(2)}, u32[]{:S(2)}) async-start(f32[1,6,256,192]{3,0,1,2:T(1,128)} %copy.20), calls=%async_computation | async-start | bytes 3145728 | tf_op jit(solution)/shard_map/all_to_all | solution.py:109
  22.4 0.0 reduce-scatter.2.cloned.1.call-start
  22.5 0.1 broadcast_multiply_fusion.2
  22.6 0.1 dynamic_slice.6
  22.7 0.2 fusion.101
  22.8 0.1 broadcast_add_fusion
  22.9 0.3 fusion.97
  23.2 21.3 %all-to-all-done = f32[1,6,256,192]{3,0,1,2:T(1,128)S(1)} async-done(((f32[1,6,256,192]{3,0,1,2:T(1,128)}), f32[1,6,256,192]{3,0,1,2:T(1,128)S(1)}, u32[]{:S(2)}, u32[]{:S(2)}) %all-to-all-start) | async-done | bytes 1179680 | tf_op jit(solution)/shard_map/all_to_all | solution.py:109
  44.5 0.1 copy.21
  44.6 0.0 slice-start
  44.7 0.9 copy.56
  45.6 0.2 add_bitcast_fusion
  45.8 0.0 slice-start.1
  45.9 0.2 fusion.11
  46.1 0.0 slice-start.2
  46.1 6.8 %fusion.12 = f32[2,16,6,128]{3,2,1,0:T(8,128)S(1)} fusion(bf16[2,8,6,16,192]{4,2,1,3,0:T(8,128)(2,1)S(1)} %fusion.11, bf16[16,2,8,192,128]{4,3,2,1,0:T(8,128)(2,1)} %bitcast.123), kind=kOutput, calls=%fused_computation.72 | convolution fusion | flops 75497472 | bytes 13271040 | tf_op jit(solution)/shard_map/mpwlk,pwcml->cpmk/dot_general | solution.py:115
  52.9 0.1 slice-done.2
  53.1 2.2 %fusion.21 = f32[6,2,16,128]{3,0,2,1:T(8,128)S(1)} fusion(f32[2,16,6,128]{3,2,1,0:T(8,128)S(1)} %fusion.12, bf16[16,2,8,192,128]{4,3,2,1,0:T(8,128)(2,1)S(1)} %bitcast.126, bf16[2,8,6,16,192]{4,2,1,3,0:T(8,128)(2,1)S(1)} %fusion.11, f32[1,8,6,16,192]{4,2,1,3,0:T(8,128)S(1)} %get-tuple-element.86, f32[1,8,6,16,192]{4,2,1,3,0:T(8,128)S(1)} %get-tuple-element.85), kind=kOutput, calls=%fused_computation.75 | convolution fusion | flops 76701696 | bytes 14548992 | tf_op jit(solution)/shard_map/mpwlk,pwcml->cpmk/dot_general | solution.py:116
  55.2 37.6 %all_gather.3 = f32[6,2,16,1024]{3,0,2,1:T(8,128)S(1)} all-gather(f32[6,2,16,128]{3,0,2,1:T(8,128)S(1)} %fusion.21), channel_id=1, replica_groups=mesh['wave'=16,'pole'=8] {'pole'}, dimensions={3}, use_global_device_ids=true | all-gather | bytes 884736 | tf_op jit(solution)/shard_map/all_gather | solution.py:121
  92.8 0.9 fusion.99
  93.7 0.1 copy_bitcast_fusion.3
  93.8 0.1 copy_bitcast_fusion.7
  93.8 0.1 copy_bitcast_fusion.5
  93.9 0.8 multiply_subtract_fusion.16
  94.7 0.2 pad_maximum_fusion.1
  95.0 0.8 fusion.110
  95.8 0.5 fusion.4
  96.3 0.9 multiply_subtract_fusion.14
  97.2 0.2 pad_maximum_fusion.2
  97.4 0.8 fusion.109
  98.3 0.5 fusion.5
  98.8 0.9 multiply_subtract_fusion.12
  99.7 0.2 pad_maximum_fusion.3
  99.9 0.8 fusion.108
  100.7 0.5 fusion.6
  101.2 0.9 multiply_subtract_fusion.10
  102.2 0.2 pad_maximum_fusion.4
  102.4 0.8 fusion.107
  103.2 0.5 fusion.7
  103.7 0.9 multiply_subtract_fusion.8
  104.6 0.2 pad_maximum_fusion.5
  104.8 1.0 fusion.106
  105.9 0.5 fusion.8
  106.4 0.9 multiply_subtract_fusion.6
  107.3 0.2 pad_maximum_fusion.6
  107.5 0.8 fusion.105
  108.3 0.5 fusion.9
  108.9 0.9 multiply_subtract_fusion.4
  109.8 0.2 pad_maximum_fusion.7
  110.0 0.8 fusion.104
  110.8 0.5 fusion.10
  111.3 0.4 multiply_subtract_fusion.2
  111.7 0.1 copy_bitcast_fusion.1
  111.8 0.7 multiply_add_fusion
  112.5 1.1 add_reduce_fusion
  113.7 0.9 copy-done.2
  114.5 0.0 reduce-scatter.2.cloned.1.call-update
  114.6 71.5 %reduce-scatter.2.cloned.1.call-done = f32[6,2,16,128]{3,2,1,0:T(8,128)} async-done(((f32[6,2,16,1024]{3,2,1,0:T(8,128)}), f32[6,2,16,128]{3,2,1,0:T(8,128)}) %reduce-scatter.2.cloned.1.call-update) | async-done | bytes 98320 | tf_op jit(solution)/shard_map/reduce_scatter | solution.py:126
  (23 shorter events, 0.1 us)
Async XLA Ops:
  6.5 16.1 %copy-start = (f32[4,64]{1,0:T(4,128)S(1)}, f32[4,64]{1,0:T(4,128)}, u32[]{:S(2)}) copy-start(f32[4,64]{1,0:T(4,128)} %param.8) | copy-start | bytes 3076
  16.2 6.2 %copy-start.3 = (s32[256]{0:T(256)S(1)}, s32[256]{0:T(256)}, u32[]{:S(2)}) copy-start(s32[256]{0:T(256)} %param.7) | copy-start | bytes 3076
  16.2 6.3 %copy-start.4 = (s32[32]{0:T(128)S(1)}, s32[32]{0:T(128)}, u32[]{:S(2)}) copy-start(s32[32]{0:T(128)} %param.9) | copy-start | bytes 388
  16.2 28.2 %all-to-all-start = ((f32[1,6,256,192]{3,0,1,2:T(1,128)}), f32[1,6,256,192]{3,0,1,2:T(1,128)S(1)}, u32[]{:S(2)}, u32[]{:S(2)}) async-start(f32[1,6,256,192]{3,0,1,2:T(1,128)} %copy.20), calls=%async_computation | async-start | bytes 3145728 | tf_op jit(solution)/shard_map/all_to_all | solution.py:109
  22.4 163.6 %reduce-scatter.2.cloned.1.call-start = ((), (), s32[]{:S(2)}) async-start(), calls=%async_computation.2 | async-start | bytes 884736 | tf_op jit(solution)/shard_map/reduce_scatter | solution.py:126
  44.6 8.3 %slice-start = ((s8[12582912]{0:T(1024)(128)(4,1)}), s8[4194304]{0:T(1024)(128)(4,1)S(1)}, s32[]{:S(2)}) async-start(s8[12582912]{0:T(1024)(128)(4,1)} %bitcast.124), calls=%async_computation.3 | async-start | bytes 8388608
  45.8 7.1 %slice-start.1 = ((s8[12582912]{0:T(1024)(128)(4,1)}), s8[4194304]{0:T(1024)(128)(4,1)S(1)}, s32[]{:S(2)}) async-start(s8[12582912]{0:T(1024)(128)(4,1)} %bitcast.124), calls=%async_computation.4 | async-start | bytes 8388608
  46.1 6.9 %slice-start.2 = ((s8[12582912]{0:T(1024)(128)(4,1)}), s8[4194304]{0:T(1024)(128)(4,1)S(1)}, s32[]{:S(2)}) async-start(s8[12582912]{0:T(1024)(128)(4,1)} %bitcast.124), calls=%async_computation.5 | async-start | bytes 8388608
  112.5 73.6 %copy-start.1 = (f32[4,64]{1,0:T(4,128)S(1)}, f32[4,64]{1,0:T(4,128)}, u32[]{:S(2)}) copy-start(f32[4,64]{1,0:T(4,128)} %param.8) | copy-start | bytes 3076
  113.7 0.9 copy-start.2
Sparse Core Ops, SparseCore 0:
  114.7 71.3 reduce-scatter.1
where the time goes:
time: 193 us
  waiting for transfers between devices  92.8 us (48%)
  blocking collectives  37.6 us (19%)
  other arithmetic  17 us (9%)
  local copies, waits for them, and re-layouts  16.4 us (8%)
  between operations  13.8 us (7%)
  matrix products  9.14 us (5%)
  starting transfers between devices  6.18 us (3%)
    reduce_scatter x1, waiting for transfers between devices, shards(): lax.psum_scatter(partial_terms, 'pole', scatter_dimension=3, tiled=True)  71.5 us
    all_gather x1, blocking collectives, shards(): whole = lax.all_gather(spectra, 'pole', axis=3, tiled=True)  37.6 us
    all_to_all x1, waiting for transfers between devices, shards(): lax.all_to_all(columns[None], 'wave', split_axis=2, concat_axis=0, tiled=...  21.3 us
    dot_general x1, matrix products, shards(): jnp.einsum('mpwlk,pwcml->cpmk', leg_blocks, high, preferred_element_type=...  6.8 us
    sub x8, other arithmetic, cmul(): return (are * bre - aim * bim, are * bim + aim * bre)  6.75 us
    all_to_all x1, starting transfers between devices, shards(): lax.all_to_all(columns[None], 'wave', split_axis=2, concat_axis=0, tiled=...  6.14 us
    slice x7, local copies, waits for them, and re-layouts, solve(): ext[:, :, 1, :, 1:count + 1]  5.96 us
    unnamed x26, local copies, waits for them, and re-layouts  4.13 us
  transfers between devices with their start and end apart: 2, of which 2 were waited for; matrix products, arithmetic and copies ran while one was open for 0% of the time, Pallas kernels for 0%

commit v1 on v0

--- a/solution.py
+++ b/solution.py
@@ -1,3 +1,4 @@
+import functools
 import jax
 import jax.numpy as jnp
 from jax import lax
@@ -6,6 +7,17 @@
 SWEEPS = 8
 coriolis_step = 1.2
 gravity_step = 0.0008
+
+
+def pack_samples_on(sheet, mesh_ax):
+    local_next = jnp.concatenate(
+        lax.all_to_all(jnp.stack([sheet for _ in range(lax.axis_size(mesh_ax))], 0), mesh_ax, 0, 0),
+        3,
+    )
+    return local_next
+
+
+block_edit = functools.partial(pack_samples_on, mesh_ax="pole")
 
 
 def split_high(values):
@@ -118,7 +130,7 @@
     own_waves = lax.dynamic_slice_in_dim(wave_table, lax.axis_index("wave") * slots, slots).astype(
         jnp.float32
     )
-    whole = lax.all_gather(spectra, "pole", axis=3, tiled=True)
+    whole = block_edit(spectra)
     per_device = pole_index.shape[0] // lax.axis_size("pole")
     chosen = lax.dynamic_slice_in_dim(pole_index, lax.axis_index("pole") * per_device, per_device)
     coef = coefficients(own_waves, whole.shape[3])

time: 193 us -> 175 us (0.907)
  blocking collectives: 37.6 us -> 0 us
  waiting for transfers between devices: 92.8 us -> 104 us
  starting transfers between devices: 6.18 us -> 13.7 us
    all_gather x1 -> x0, blocking collectives: 37.6 us -> none  [shards(): whole = lax.all_gather(spectra, 'pole', axis=3, tiled=True)]
    all_to_all x0 -> x1, waiting for transfers between devices: none -> 12.5 us  [pack_samples_on(): lax.all_to_all(jnp.stack([sheet for _ in range(lax.axis_size(mesh_ax))],...]
    all_to_all x0 -> x1, starting transfers between devices: none -> 7.32 us  [pack_samples_on(): lax.all_to_all(jnp.stack([sheet for _ in range(lax.axis_size(mesh_ax))],...]
    unnamed x26 -> x22, local copies, waits for them, and re-layouts: 4.13 us -> 3.93 us
  transfers between devices with their start and end apart: 2 -> 3, of which waited for: 2 -> 3; matrix products, arithmetic and copies ran while one was open for 0% -> 0% of each run, Pallas kernels for 0% -> 0%
where the time goes in v1:
time: 175 us
  waiting for transfers between devices  104 us (59%)
  local copies, waits for them, and re-layouts  17.7 us (10%)
  other arithmetic  16.4 us (9%)
  between operations  13.9 us (8%)
  starting transfers between devices  13.7 us (8%)
  matrix products  9.14 us (5%)
    reduce_scatter x1, waiting for transfers between devices, shards(): lax.psum_scatter(partial_terms, 'pole', scatter_dimension=3, tiled=True)  69.8 us
    all_to_all x1, waiting for transfers between devices, shards(): lax.all_to_all(columns[None], 'wave', split_axis=2, concat_axis=0, tiled=...  22 us
    all_to_all x1, waiting for transfers between devices, pack_samples_on(): lax.all_to_all(jnp.stack([sheet for _ in range(lax.axis_size(mesh_ax))],...  12.5 us
    all_to_all x1, starting transfers between devices, pack_samples_on(): lax.all_to_all(jnp.stack([sheet for _ in range(lax.axis_size(mesh_ax))],...  7.32 us
    dot_general x1, matrix products, shards(): jnp.einsum('mpwlk,pwcml->cpmk', leg_blocks, high, preferred_element_type=...  6.8 us
    sub x8, other arithmetic, cmul(): return (are * bre - aim * bim, are * bim + aim * bre)  6.75 us
    all_to_all x1, starting transfers between devices, shards(): lax.all_to_all(columns[None], 'wave', split_axis=2, concat_axis=0, tiled=...  6.14 us
    slice x7, local copies, waits for them, and re-layouts, solve(): ext[:, :, 1, :, 1:count + 1]  5.75 us
  transfers between devices with their start and end apart: 3, of which 3 were waited for; matrix products, arithmetic and copies ran while one was open for 0% of the time, Pallas kernels for 0%

profile of v1, /device:TPU:0, one launch (start us, length us, event | category | flops | bytes accessed | tf_op | source)
XLA Modules:
  0.0 175.1 jit_solution(3673953221735133096)
XLA Ops:
  6.5 0.7 compare_and_fusion
  7.2 0.7 compare_select_fusion
  7.9 2.8 %copy.35 = f32[6,256,192]{2,0,1:T(8,128)} copy(f32[6,256,192]{1,2,0:T(8,128)} %param.5) | data formatting | bytes 2359296 | tf_op args[0]
  10.8 2.3 %gather_fusion = f32[256,6,192]{2,1,0:T(8,128)S(1)} fusion(f32[6,256,192]{2,0,1:T(8,128)} %copy.35, s32[1024]{0:T(1024)S(1)} %pad_clamp_fusion), kind=kCustom, calls=%fused_computation | custom fusion | bytes 2360320 | tf_op jit(solution)/shard_map/jit(_take)/gather | solution.py:120
  13.1 0.3 bitcast_select_fusion
  13.5 2.8 %copy.36 = f32[1,6,256,192]{3,0,1,2:T(1,128)} copy(f32[1,6,256,192]{3,1,2,0:T(8,128)S(1)} %bitcast_select_fusion) | data formatting | bytes 2359296 | tf_op jit(solution)/shard_map/jit(_take)/select_n | solution.py:120
  16.3 6.1 %all-to-all-start = ((f32[1,6,256,192]{3,0,1,2:T(1,128)}), f32[1,6,256,192]{3,0,1,2:T(1,128)S(1)}, u32[]{:S(2)}, u32[]{:S(2)}) async-start(f32[1,6,256,192]{3,0,1,2:T(1,128)} %copy.36), calls=%async_computation | async-start | bytes 3145728 | tf_op jit(solution)/shard_map/all_to_all | solution.py:121
  22.4 0.1 broadcast_multiply_fusion.2
  22.5 22.0 %all-to-all-done = f32[1,6,256,192]{3,0,1,2:T(1,128)S(1)} async-done(((f32[1,6,256,192]{3,0,1,2:T(1,128)}), f32[1,6,256,192]{3,0,1,2:T(1,128)S(1)}, u32[]{:S(2)}, u32[]{:S(2)}) %all-to-all-start) | async-done | bytes 1179680 | tf_op jit(solution)/shard_map/all_to_all | solution.py:121
  44.5 0.1 copy.37
  44.7 0.9 copy.63
  45.6 0.2 add_bitcast_fusion
  45.9 0.2 fusion.11
  46.1 6.8 %fusion.12 = f32[2,16,6,128]{3,2,1,0:T(8,128)S(1)} fusion(bf16[2,8,6,16,192]{4,2,1,3,0:T(8,128)(2,1)S(1)} %fusion.11, bf16[16,2,8,192,128]{4,3,2,1,0:T(8,128)(2,1)} %bitcast.120), kind=kOutput, calls=%fused_computation.72 | convolution fusion | flops 75497472 | bytes 13271040 | tf_op jit(solution)/shard_map/mpwlk,pwcml->cpmk/dot_general | solution.py:127
  53.0 0.1 slice-done.2
  53.1 2.2 %fusion.21 = f32[6,2,16,128]{3,0,2,1:T(8,128)S(1)} fusion(f32[2,16,6,128]{3,2,1,0:T(8,128)S(1)} %fusion.12, bf16[16,2,8,192,128]{4,3,2,1,0:T(8,128)(2,1)S(1)} %bitcast.123, bf16[2,8,6,16,192]{4,2,1,3,0:T(8,128)(2,1)S(1)} %fusion.11, f32[1,8,6,16,192]{4,2,1,3,0:T(8,128)S(1)} %get-tuple-element.86, f32[1,8,6,16,192]{4,2,1,3,0:T(8,128)S(1)} %get-tuple-element.85), kind=kOutput, calls=%fused_computation.75 | convolution fusion | flops 76701696 | bytes 14548992 | tf_op jit(solution)/shard_map/mpwlk,pwcml->cpmk/dot_general | solution.py:128
  55.3 1.0 stack.61
  56.2 7.3 %all-to-all-start.1 = ((f32[8,6,2,16,128]{4,3,2,1,0:T(8,128)}), f32[8,6,2,16,128]{4,3,2,1,0:T(8,128)S(1)}, u32[]{:S(2)}, u32[]{:S(2)}) async-start(f32[8,6,2,16,128]{4,3,2,1,0:T(8,128)} %stack.61), calls=%async_computation.1 | async-start | bytes 1572864 | tf_op jit(solution)/shard_map/all_to_all | solution.py:14
  63.6 0.2 reduce-scatter.2.cloned.1.call-start
  63.8 0.1 dynamic_slice.6
  63.9 0.2 fusion.99
  64.1 0.1 broadcast_add_fusion
  64.2 12.5 %all-to-all-done.1 = f32[8,6,2,16,128]{4,3,2,1,0:T(8,128)S(1)} async-done(((f32[8,6,2,16,128]{4,3,2,1,0:T(8,128)}), f32[8,6,2,16,128]{4,3,2,1,0:T(8,128)S(1)}, u32[]{:S(2)}, u32[]{:S(2)}) %all-to-all-start.1) | async-done | bytes 786464 | tf_op jit(solution)/shard_map/all_to_all | solution.py:14
  76.7 0.1 fusion.109
  76.8 0.1 copy.42
  76.9 0.1 copy.47
  77.0 0.1 copy.46
  77.1 0.1 copy.45
  77.3 0.1 copy.44
  77.4 0.1 copy.43
  77.5 0.3 fusion.87
  77.8 0.8 multiply_subtract_fusion.16
  78.6 0.2 pad_maximum_fusion.1
  78.8 0.8 fusion.108
  79.7 0.5 fusion.4
  80.2 0.9 multiply_subtract_fusion.14
  81.1 0.2 pad_maximum_fusion.2
  81.3 0.8 fusion.107
  82.2 0.5 fusion.5
  82.7 0.9 multiply_subtract_fusion.12
  83.6 0.2 pad_maximum_fusion.3
  83.8 0.8 fusion.106
  84.6 0.5 fusion.6
  85.2 0.9 multiply_subtract_fusion.10
  86.1 0.2 pad_maximum_fusion.4
  86.3 0.8 fusion.105
  87.1 0.5 fusion.7
  87.7 0.9 multiply_subtract_fusion.8
  88.6 0.2 pad_maximum_fusion.5
  88.8 0.8 fusion.104
  89.6 0.7 fusion.8
  90.3 0.9 multiply_subtract_fusion.6
  91.3 0.2 pad_maximum_fusion.6
  91.5 0.8 fusion.103
  92.3 0.5 fusion.9
  92.8 0.9 multiply_subtract_fusion.4
  93.8 0.2 pad_maximum_fusion.7
  93.9 0.8 fusion.102
  94.8 0.5 fusion.10
  95.3 0.4 multiply_subtract_fusion.2
  95.7 0.7 multiply_add_fusion
  96.4 1.1 add_reduce_fusion
  97.6 0.9 copy-done.2
  98.5 69.8 %reduce-scatter.2.cloned.1.call-done = f32[6,2,16,128]{3,2,1,0:T(8,128)} async-done(((f32[6,2,16,1024]{3,2,1,0:T(8,128)}), f32[6,2,16,128]{3,2,1,0:T(8,128)}) %reduce-scatter.2.cloned.1.call-update) | async-done | bytes 98320 | tf_op jit(solution)/shard_map/reduce_scatter | solution.py:138
  (34 shorter events, 0.4 us)
Async XLA Ops:
  6.5 57.4 %copy-start = (f32[4,64]{1,0:T(4,128)S(1)}, f32[4,64]{1,0:T(4,128)}, u32[]{:S(2)}) copy-start(f32[4,64]{1,0:T(4,128)} %param.8) | copy-start | bytes 3076
  16.3 6.2 %copy-start.3 = (s32[256]{0:T(256)S(1)}, s32[256]{0:T(256)}, u32[]{:S(2)}) copy-start(s32[256]{0:T(256)} %param.7) | copy-start | bytes 3076
  16.3 28.2 %all-to-all-start = ((f32[1,6,256,192]{3,0,1,2:T(1,128)}), f32[1,6,256,192]{3,0,1,2:T(1,128)S(1)}, u32[]{:S(2)}, u32[]{:S(2)}) async-start(f32[1,6,256,192]{3,0,1,2:T(1,128)} %copy.36), calls=%async_computation | async-start | bytes 3145728 | tf_op jit(solution)/shard_map/all_to_all | solution.py:121
  44.7 8.3 %slice-start = ((s8[12582912]{0:T(1024)(128)(4,1)}), s8[4194304]{0:T(1024)(128)(4,1)S(1)}, s32[]{:S(2)}) async-start(s8[12582912]{0:T(1024)(128)(4,1)} %bitcast.121), calls=%async_computation.4 | async-start | bytes 8388608
  45.9 7.1 %slice-start.1 = ((s8[12582912]{0:T(1024)(128)(4,1)}), s8[4194304]{0:T(1024)(128)(4,1)S(1)}, s32[]{:S(2)}) async-start(s8[12582912]{0:T(1024)(128)(4,1)} %bitcast.121), calls=%async_computation.5 | async-start | bytes 8388608
  46.1 6.9 %slice-start.2 = ((s8[12582912]{0:T(1024)(128)(4,1)}), s8[4194304]{0:T(1024)(128)(4,1)S(1)}, s32[]{:S(2)}) async-start(s8[12582912]{0:T(1024)(128)(4,1)} %bitcast.121), calls=%async_computation.6 | async-start | bytes 8388608
  55.2 8.6 %copy-start.4 = (s32[32]{0:T(128)S(1)}, s32[32]{0:T(128)}, u32[]{:S(2)}) copy-start(s32[32]{0:T(128)} %param.9) | copy-start | bytes 388
  56.2 20.5 %all-to-all-start.1 = ((f32[8,6,2,16,128]{4,3,2,1,0:T(8,128)}), f32[8,6,2,16,128]{4,3,2,1,0:T(8,128)S(1)}, u32[]{:S(2)}, u32[]{:S(2)}) async-start(f32[8,6,2,16,128]{4,3,2,1,0:T(8,128)} %stack.61), calls=%async_computation.1 | async-start | bytes 1572864 | tf_op jit(solution)/shard_map/all_to_all | solution.py:14
  63.6 104.7 %reduce-scatter.2.cloned.1.call-start = ((), (), s32[]{:S(2)}) async-start(), calls=%async_computation.3 | async-start | bytes 884736 | tf_op jit(solution)/shard_map/reduce_scatter | solution.py:138
  96.4 71.9 %copy-start.1 = (f32[4,64]{1,0:T(4,128)S(1)}, f32[4,64]{1,0:T(4,128)}, u32[]{:S(2)}) copy-start(f32[4,64]{1,0:T(4,128)} %param.8) | copy-start | bytes 3076
  97.6 0.9 copy-start.2
Sparse Core Ops, SparseCore 0:
  98.6 69.6 reduce-scatter.1
